TPU v7x, 32 devices: a whole 2x2x4 slice. The times are simulated.
32 devices in a mesh: tile: 8 (over z, y), win: 4 (over x, core).
Axes of the slice: x: 2, y: 2, z: 4, core: 2. Of those that a mesh axis runs over, the one named last changes fastest.
Arguments:
- records: bfloat16 [16, 2048, 2048], P('win', 'tile'), may hold values from -6 to 6
- pair_first: int32 [2048], P('tile'), may hold values from 0 to 255
- pair_offset: int32 [2048], P('tile'), may hold values from 1 to 255
- owners: int32 [2048, 1], P('tile'), may hold values from 0 to 7; in each aligned block of 256 rows (0 to 255, 256 to 511, ...) at most 80 rows name the same one
Outputs:
- gathers: bfloat16 [8, 8, 80, 2048], P('tile', None, None, 'win')
Inputs may be any that keep to these rules, and one draw needn't show every extreme that they name: `owners`: among the 256 pairs of one tile no owner is named more than 80 times, and in every draw some tile names some owner exactly 80 times.
All inputs are finite; a program needn't handle non-finite values.
Results may differ from a plain program's by a relative error of at most 0.0066.
Values may be sent and summed in bfloat16 or wider, within the bound.
No kernel may reach another device: no remote copies, remote signals or barrier semaphores. Data moves between devices by JAX's collectives and lax.ppermute only.
A program may use at most 128 MiB of HBM per device.

v0:
```python
import math
import jax
import jax.numpy as jnp
from jax import lax
from jax.sharding import PartitionSpec as P

BAND = 64
power_floor = 1e-06


def passed_along(block, axis, distance):
    devices = range(lax.axis_size(axis))
    route = [((i - distance) % len(devices), i) for i in devices]
    return lax.ppermute(block, axis, route)


def forward_matrix(length):
    row_index = lax.broadcasted_iota(jnp.int32, (length // 2, length), 0)
    col_index = lax.broadcasted_iota(jnp.int32, (length // 2, length), 1)
    phases = row_index * col_index % length
    angles = phases.astype(jnp.float32) * (2.0 * math.pi / length)
    return jnp.concatenate([jnp.cos(angles), -jnp.sin(angles)], axis=0).astype(jnp.bfloat16)


def inverse_matrix(length, first_lag, lag_count, seg_total):
    half_bins = length // 2
    lag_index = lax.broadcasted_iota(jnp.int32, (lag_count, half_bins), 0) + first_lag
    bin_index = lax.broadcasted_iota(jnp.int32, (lag_count, half_bins), 1)
    phases = lag_index * bin_index % length
    angles = phases.astype(jnp.float32) * (2.0 * math.pi / length)
    weights = jnp.where(bin_index == 0, 1.0, 2.0).astype(jnp.float32) * (
        1.0 / math.sqrt(half_bins * seg_total)
    )
    return jnp.concatenate([weights * jnp.cos(angles), -weights * jnp.sin(angles)], axis=1)


def whiten(spectra, band_width):
    half_bins = spectra.shape[-2] // 2
    real_rows = spectra[..., :half_bins, :]
    imaginary = spectra[..., half_bins:, :]
    energy = real_rows * real_rows + imaginary * imaginary
    grouped = energy.shape[:-2] + (half_bins // band_width, band_width, energy.shape[-1])
    band_power = jnp.mean(energy.reshape(grouped), axis=-2, keepdims=True)
    inverse_rms = jnp.broadcast_to(lax.rsqrt(band_power + power_floor), grouped).reshape(
        energy.shape
    )
    return (spectra * jnp.concatenate([inverse_rms, inverse_rms], axis=-2)).astype(jnp.bfloat16)


def cross_terms(first_part, second_part):
    half_bins = first_part.shape[-2] // 2
    first_real = first_part[..., :half_bins, :].astype(jnp.float32)
    first_imag = first_part[..., half_bins:, :].astype(jnp.float32)
    second_real = second_part[..., :half_bins, :].astype(jnp.float32)
    second_imag = second_part[..., half_bins:, :].astype(jnp.float32)
    real_sum = first_real * second_real + first_imag * second_imag
    imag_sum = first_imag * second_real - first_real * second_imag
    return jnp.concatenate([real_sum, imag_sum], axis=-2)


def bucket_select(owner_ids, owner_count, capacity):
    onehot = (owner_ids[:, None] == jnp.arange(owner_count, dtype=jnp.int32)[None, :]).astype(
        jnp.int32
    )
    slot_rank = jnp.sum((jnp.cumsum(onehot, axis=0, dtype=jnp.int32) - 1) * onehot, axis=1)
    slot_id = owner_ids * capacity + slot_rank
    return (
        slot_id[None, :] == jnp.arange(owner_count * capacity, dtype=jnp.int32)[:, None]
    ).astype(jnp.bfloat16)


def per_device(records, pair_first, pair_offset, owners):
    tile_count = lax.axis_size("tile")
    win_count = lax.axis_size("win")
    length = records.shape[1] * tile_count
    seg_total = records.shape[0] * win_count
    forward = forward_matrix(length)
    spectra = jnp.einsum(
        "fn,snc->sfc",
        forward,
        lax.all_to_all(records, "tile", split_axis=2, concat_axis=1, tiled=True),
        preferred_element_type=jnp.float32,
    )
    whitened = whiten(spectra, BAND)
    following = passed_along(whitened, "tile", -1)
    joined = jnp.concatenate([whitened, following], axis=2)
    first_part = jnp.take(joined, pair_first, axis=2)
    second_part = jnp.take(joined, pair_first + pair_offset, axis=2)
    cross = jnp.sum(cross_terms(first_part, second_part), axis=0)
    lag_count = length // win_count
    stacked = lax.psum(cross, "win")
    inverse = inverse_matrix(length, lax.axis_index("win") * lag_count, lag_count, seg_total)
    correlation = jnp.dot(inverse, stacked, precision=lax.Precision.HIGHEST)
    capacity = 5 * pair_first.shape[0] // (2 * tile_count)
    chooser = bucket_select(owners[:, 0], tile_count, capacity)
    picked = lax.dot_general(
        chooser,
        correlation.astype(jnp.bfloat16),
        (((1,), (1,)), ((), ())),
        preferred_element_type=jnp.float32,
    )
    buckets = picked.astype(jnp.bfloat16).reshape(tile_count, capacity, lag_count)
    received = lax.all_to_all(buckets, "tile", split_axis=0, concat_axis=0, tiled=True)
    return received[None]


def solution(mesh):
    placed = (P("win", "tile", None), P("tile"), P("tile"), P("tile", None))
    return jax.shard_map(
        per_device,
        mesh=mesh,
        in_specs=placed,
        out_specs=P("tile", None, None, "win"),
        check_vma=False,
    )
```

profile of v0, /device:TPU:0, one launch (start us, length us, event | category | flops | bytes accessed | tf_op | source)
XLA Modules:
  0.0 394.3 jit_solution(4413621781152123788)
XLA Ops:
  6.5 7.5 %copy.9 = bf16[4,256,2048]{1,0,2:T(4,128)(2,1)} copy(bf16[4,256,2048]{2,1,0:T(8,128)(2,1)} %param.6) | data formatting | bytes 8388608 | tf_op args[0]
  14.0 7.3 %all-to-all-start = ((bf16[4,256,2048]{1,0,2:T(4,128)(2,1)}), bf16[4,256,2048]{1,0,2:T(4,128)(2,1)}, u32[]{:S(2)}, u32[]{:S(2)}) async-start(bf16[4,256,2048]{1,0,2:T(4,128)(2,1)} %copy.9), calls=%async_computation | async-start | bytes 8388608 | tf_op jit(solution)/shard_map/all_to_all | solution.py:81
  21.3 34.8 %negate_convert_fusion = (bf16[1024,2048]{1,0:T(8,128)(2,1)}, bf16[1024,2048]{1,0:T(8,128)(2,1)}) fusion(), kind=kLoop, calls=%fused_computation.16 | loop fusion | flops 35651584 | bytes 8388608 | tf_op jit(solution)/shard_map/convert.1
  56.1 58.5 %all-to-all-done = bf16[4,256,2048]{1,0,2:T(4,128)(2,1)} async-done(((bf16[4,256,2048]{1,0,2:T(4,128)(2,1)}), bf16[4,256,2048]{1,0,2:T(4,128)(2,1)}, u32[]{:S(2)}, u32[]{:S(2)}) %all-to-all-start) | async-done | bytes 4194336 | tf_op jit(solution)/shard_map/all_to_all | solution.py:81
  114.6 7.5 %copy.10 = bf16[4,256,8,256]{3,1,2,0:T(8,128)(2,1)} copy(bf16[4,256,8,256]{1,0,3,2:T(4,128)(2,1)} %bitcast.5) | data formatting | bytes 8388608 | tf_op jit(solution)/shard_map/all_to_all | solution.py:81
  122.1 12.4 %fusion.10 = f32[4,2048,256]{2,1,0:T(8,128)S(1)} fusion(bf16[4,2048,256]{2,1,0:T(8,128)(2,1)} %bitcast.32, bf16[1024,2048]{1,0:T(8,128)(2,1)} %get-tuple-element.13, bf16[1024,2048]{1,0:T(8,128)(2,1)} %get-tuple-element.14), kind=kOutput, calls=%fused_computation.25 | convolution fusion | flops 8606711808 | bytes 20971520 | tf_op jit(solution)/shard_map/fn,snc->sfc/dot_general | solution.py:78
  134.5 1.2 bitcast_reduce_fusion
  136.1 1.2 fusion.6
  137.4 1.9 copy-done.1
  139.3 2.4 collective-permute-start
  141.7 89.9 %collective-permute-done = bf16[4,2048,256]{2,1,0:T(8,128)(2,1)} collective-permute-done((bf16[4,2048,256]{2,1,0:T(8,128)(2,1)S(1)}, bf16[4,2048,256]{2,1,0:T(8,128)(2,1)}, u32[]{:S(2)}, u32[]{:S(2)}) %collective-permute-start) | collective-permute-done | bytes 4194336 | tf_op jit(solution)/shard_map/ppermute | solution.py:14
  231.7 7.3 %pad_maximum_fusion = bf16[4,2048,512]{2,1,0:T(8,128)(2,1)} fusion(bf16[4,2048,256]{2,1,0:T(8,128)(2,1)} %collective-permute-done, bf16[4,2048,256]{2,1,0:T(8,128)(2,1)} %copy-done.1), kind=kLoop, calls=%fused_computation.14 | loop fusion | flops 16777216 | bytes 16777216 | tf_op jit(solution)/shard_map/concatenate | solution.py:86
  239.0 14.9 %copy.11 = bf16[4,2048,512]{1,0,2:T(4,128)(2,1)} copy(bf16[4,2048,512]{2,1,0:T(8,128)(2,1)} %pad_maximum_fusion) | data formatting | bytes 16777216 | tf_op jit(solution)/shard_map/concatenate | solution.py:86
  253.9 13.3 %gather_fusion.1 = bf16[256,4,2048]{2,1,0:T(4,128)(2,1)} fusion(bf16[4,2048,512]{1,0,2:T(4,128)(2,1)} %copy.11, s32[1024]{0:T(1024)S(1)} %pad_clamp_fusion), kind=kCustom, calls=%fused_computation.1.clone | custom fusion | bytes 8389632 | tf_op jit(solution)/shard_map/jit(_take)/gather | solution.py:88
  267.1 13.3 %gather_fusion = bf16[256,4,2048]{2,1,0:T(4,128)(2,1)} fusion(bf16[4,2048,512]{1,0,2:T(4,128)(2,1)} %copy.11, s32[1024]{0:T(1024)S(1)} %pad_clamp_fusion.1), kind=kCustom, calls=%fused_computation.clone | custom fusion | bytes 8389632 | tf_op jit(solution)/shard_map/jit(_take)/gather | solution.py:87
  280.5 4.4 %select_bitcast_fusion = bf16[4,2048,256]{1,0,2:T(4,128)(2,1)S(1)} fusion(bf16[256,4,2048]{2,1,0:T(4,128)(2,1)} %gather_fusion.1, pred[256]{0:T(512)(128)(4,1)S(1)} %get-tuple-element.6), kind=kLoop, calls=%fused_computation.36 | loop fusion | flops 2097152 | bytes 8388864 | tf_op jit(solution)/shard_map/jit(_take)/select_n | solution.py:88
  284.9 1.9 select_bitcast_fusion.1
  286.8 6.4 %fusion.11 = (f32[4,1024,256]{1,0,2:T(4,128)}, f32[4,1024,256]{1,0,2:T(4,128)}) fusion(bf16[4,2048,256]{1,0,2:T(4,128)(2,1)S(1)} %select_bitcast_fusion, bf16[4,2048,256]{1,0,2:T(4,128)(2,1)S(1)} %select_bitcast_fusion.1), kind=kLoop, calls=%fused_computation.26 | loop fusion | flops 10485760 | bytes 16777216 | tf_op jit(solution)/shard_map/add | solution.py:56
  293.3 11.0 %maximum_reduce_fusion = f32[2048,256]{0,1:T(8,128)} fusion(f32[4,1024,256]{1,0,2:T(4,128)} %get-tuple-element.9, f32[4,1024,256]{1,0,2:T(4,128)} %get-tuple-element.8), kind=kLoop, calls=%fused_computation.15 | loop fusion | flops 3670016 | bytes 10485760 | tf_op jit(solution)/shard_map/reduce_sum | solution.py:89
  305.3 9.8 %cosine_multiply_fusion = (f32[512,1024]{1,0:T(8,128)S(1)}, f32[512,1024]{1,0:T(8,128)}) fusion(s32[512]{0:T(512)S(1)} %iota_add_fusion, f32[1024]{0:T(1024)S(1)} %get-tuple-element.15, f32[1024]{0:T(1024)S(1)} %get-tuple-element.16), kind=kLoop, calls=%fused_computation.45 | loop fusion | flops 8388608 | bytes 4204544 | tf_op jit(solution)/shard_map/mul | solution.py:34
  315.1 42.7 %all-reduce.2.cloned.1.call-done = f32[2048,256]{0,1:T(8,128)} async-done(((f32[2048,256]{0,1:T(8,128)}), f32[2048,256]{0,1:T(8,128)}) %all-reduce.2.cloned.1.call-update) | async-done | bytes 2097168 | tf_op jit(solution)/shard_map/psum | solution.py:91
  357.8 5.7 %fusion.24 = bf16[512,256]{1,0:T(8,128)(2,1)S(1)} fusion(f32[2048,256]{0,1:T(8,128)} %all-reduce.2.cloned.1.call-done, f32[512,1024]{1,0:T(8,128)} %get-tuple-element.11, f32[512,1024]{1,0:T(8,128)S(1)} %get-tuple-element.10), kind=kOutput, calls=%fused_computation.50 | convolution fusion | flops 3222405120 | bytes 6553600 | tf_op jit(solution)/shard_map/dot_general | solution.py:93
  363.9 22.8 %all_to_all.23 = bf16[8,80,512]{2,1,0:T(8,128)(2,1)S(1)} all-to-all(bf16[8,80,512]{2,1,0:T(8,128)(2,1)S(1)} %bitcast.33), channel_id=1, replica_groups=mesh['tile'=8,'win'=4] {'tile'}, dimensions={0} | all-to-all | bytes 1310720 | tf_op jit(solution)/shard_map/all_to_all | solution.py:103
  386.7 0.8 copy.15
  (27 shorter events, 1.8 us)
Async XLA Ops:
  14.0 100.6 %all-to-all-start = ((bf16[4,256,2048]{1,0,2:T(4,128)(2,1)}), bf16[4,256,2048]{1,0,2:T(4,128)(2,1)}, u32[]{:S(2)}, u32[]{:S(2)}) async-start(bf16[4,256,2048]{1,0,2:T(4,128)(2,1)} %copy.9), calls=%async_computation | async-start | bytes 8388608 | tf_op jit(solution)/shard_map/all_to_all | solution.py:81
  21.3 336.5 %all-reduce.2.cloned.1.call-start = ((), (), s32[]{:S(2)}) async-start(), calls=%async_computation.2 | async-start | bytes 4194304 | tf_op jit(solution)/shard_map/psum | solution.py:91
  136.1 5.6 %copy-start.3 = (s32[256]{0:T(256)S(1)}, s32[256]{0:T(256)}, u32[]{:S(2)}) copy-start(s32[256]{0:T(256)} %param.7) | copy-start | bytes 3076
  136.1 5.6 %copy-start.4 = (s32[256]{0:T(256)S(1)}, s32[256]{0:T(256)}, u32[]{:S(2)}) copy-start(s32[256]{0:T(256)} %param.8) | copy-start | bytes 3076
  137.3 2.0 copy-start.1
  139.3 92.4 %collective-permute-start = (bf16[4,2048,256]{2,1,0:T(8,128)(2,1)S(1)}, bf16[4,2048,256]{2,1,0:T(8,128)(2,1)}, u32[]{:S(2)}, u32[]{:S(2)}) collective-permute-start(bf16[4,2048,256]{2,1,0:T(8,128)(2,1)S(1)} %fusion.6), channel_id=1, source_target_pairs={{4,0},{8,4},{12,8},{16,12},{20,16},{24,20},{28,24},{0,28},{5,1},{9... | collective-permute-start | bytes 12582920 | tf_op jit(solution)/shard_map/ppermute | solution.py:14
  280.5 4.4 %copy-start = (bf16[256,4,2048]{2,1,0:T(4,128)(2,1)S(1)}, bf16[256,4,2048]{2,1,0:T(4,128)(2,1)}, u32[]{:S(2)}) copy-start(bf16[256,4,2048]{2,1,0:T(4,128)(2,1)} %gather_fusion) | copy-start | bytes 12582916
  293.3 11.0 %copy-start.2 = (s32[256,1]{0,1:T(1,128)S(1)}, s32[256,1]{0,1:T(1,128)}, u32[]{:S(2)}) copy-start(s32[256,1]{0,1:T(1,128)} %param.9) | copy-start | bytes 3076
Sparse Core Ops, SparseCore 0:
  304.4 53.3 all-reduce.1
where the time goes:
time: 395 us; the launch traced here: 394 us
  waiting for transfers between devices  191 us (48%)
  other arithmetic  78.8 us (20%)
  local copies, waits for them, and re-layouts  59.8 us (15%)
  blocking collectives  22.8 us (6%)
  matrix products  18.5 us (5%)
  between operations  13.6 us (3%)
  starting transfers between devices  9.72 us (2%)
    ppermute x1, waiting for transfers between devices, passed_along(): return lax.ppermute(block, axis, route)  89.9 us
    all_to_all x1, waiting for transfers between devices, per_device(): lax.all_to_all(records, 'tile', split_axis=2, concat_axis=1, tiled=True)  58.5 us
    psum x1, waiting for transfers between devices, per_device(): stacked = lax.psum(cross, 'win')  42.7 us
    another operation x3, other arithmetic  35.4 us
    all_to_all x1, blocking collectives, per_device(): lax.all_to_all(buckets, 'tile', split_axis=0, concat_axis=0, tiled=True)  22.8 us
    concatenate x1, local copies, waits for them, and re-layouts, per_device(): joined = jnp.concatenate([whitened, following], axis=2)  14.9 us
    gather x1, local copies, waits for them, and re-layouts, per_device(): first_part = jnp.take(joined, pair_first, axis=2)  13.3 us
    gather x1, local copies, waits for them, and re-layouts, per_device(): second_part = jnp.take(joined, pair_first + pair_offset, axis=2)  13.3 us
  transfers between devices with their start and end apart: 3, of which 3 were waited for; matrix products, arithmetic and copies ran while one was open for 12% of the time, Pallas kernels for 0%

commit v1 on v0

--- a/solution.py
+++ b/solution.py
@@ -88,7 +88,7 @@
     second_part = jnp.take(joined, pair_first + pair_offset, axis=2)
     cross = jnp.sum(cross_terms(first_part, second_part), axis=0)
     lag_count = length // win_count
-    stacked = lax.psum(cross, "win")
+    stacked = jnp.sum(lax.all_gather(cross, "win"), axis=0)
     inverse = inverse_matrix(length, lax.axis_index("win") * lag_count, lag_count, seg_total)
     correlation = jnp.dot(inverse, stacked, precision=lax.Precision.HIGHEST)
     capacity = 5 * pair_first.shape[0] // (2 * tile_count)

time: 395 us -> 430 us (1.089); the launches traced: 394 us -> 424 us
  local copies, waits for them, and re-layouts: 59.8 us -> 71.3 us
  other arithmetic: 78.8 us -> 88.7 us
  waiting for transfers between devices: 191 us -> 198 us
    all_gather x0 -> x1, waiting for transfers between devices: none -> 49.6 us  [per_device(): stacked = jnp.sum(lax.all_gather(cross, 'win'), axis=0)]
    psum x1 -> x0, waiting for transfers between devices: 42.7 us -> none  [per_device(): stacked = lax.psum(cross, 'win')]
    all_gather x0 -> x1, local copies, waits for them, and re-layouts: none -> 11 us  [per_device(): stacked = jnp.sum(lax.all_gather(cross, 'win'), axis=0)]
    reduce_sum x0 -> x1, other arithmetic: none -> 10 us  [per_device(): stacked = jnp.sum(lax.all_gather(cross, 'win'), axis=0)]
  transfers between devices with their start and end apart: 3 -> 3, of which waited for: 3 -> 3; matrix products, arithmetic and copies ran while one was open for 12% -> 11% of each run, Pallas kernels for 0% -> 0%
where the time goes in v1:
time: 430 us; the launch traced here: 424 us
  waiting for transfers between devices  198 us (46%)
  other arithmetic  88.7 us (21%)
  local copies, waits for them, and re-layouts  71.3 us (17%)
  blocking collectives  23.4 us (5%)
  matrix products  18.5 us (4%)
  between operations  13.8 us (3%)
  starting transfers between devices  9.71 us (2%)
    ppermute x1, waiting for transfers between devices, passed_along(): return lax.ppermute(block, axis, route)  90 us
    all_to_all x1, waiting for transfers between devices, per_device(): lax.all_to_all(records, 'tile', split_axis=2, concat_axis=1, tiled=True)  58.5 us
    all_gather x1, waiting for transfers between devices, per_device(): stacked = jnp.sum(lax.all_gather(cross, 'win'), axis=0)  49.6 us
    another operation x3, other arithmetic  35.4 us
    all_to_all x1, blocking collectives, per_device(): lax.all_to_all(buckets, 'tile', split_axis=0, concat_axis=0, tiled=True)  23.4 us
    concatenate x1, local copies, waits for them, and re-layouts, per_device(): joined = jnp.concatenate([whitened, following], axis=2)  15.3 us
    gather x1, local copies, waits for them, and re-layouts, per_device(): first_part = jnp.take(joined, pair_first, axis=2)  13.3 us
    gather x1, local copies, waits for them, and re-layouts, per_device(): second_part = jnp.take(joined, pair_first + pair_offset, axis=2)  13.3 us
  transfers between devices with their start and end apart: 3, of which 3 were waited for; matrix products, arithmetic and copies ran while one was open for 11% of the time, Pallas kernels for 0%

profile of v1, /device:TPU:0, one launch (start us, length us, event | category | flops | bytes accessed | tf_op | source)
XLA Modules:
  0.0 423.5 jit_solution(16327350542673408067)
XLA Ops:
  6.5 7.5 %copy.13 = bf16[4,256,2048]{1,0,2:T(4,128)(2,1)} copy(bf16[4,256,2048]{2,1,0:T(8,128)(2,1)} %param.6) | data formatting | bytes 8388608 | tf_op args[0]
  14.0 7.3 %all-to-all-start = ((bf16[4,256,2048]{1,0,2:T(4,128)(2,1)}), bf16[4,256,2048]{1,0,2:T(4,128)(2,1)}, u32[]{:S(2)}, u32[]{:S(2)}) async-start(bf16[4,256,2048]{1,0,2:T(4,128)(2,1)} %copy.13), calls=%async_computation | async-start | bytes 8388608 | tf_op jit(solution)/shard_map/all_to_all | solution.py:81
  21.3 34.8 %negate_convert_fusion = (bf16[1024,2048]{1,0:T(8,128)(2,1)}, bf16[1024,2048]{1,0:T(8,128)(2,1)}) fusion(), kind=kLoop, calls=%fused_computation.16 | loop fusion | flops 35651584 | bytes 8388608 | tf_op jit(solution)/shard_map/convert.1
  56.1 58.5 %all-to-all-done = bf16[4,256,2048]{1,0,2:T(4,128)(2,1)} async-done(((bf16[4,256,2048]{1,0,2:T(4,128)(2,1)}), bf16[4,256,2048]{1,0,2:T(4,128)(2,1)}, u32[]{:S(2)}, u32[]{:S(2)}) %all-to-all-start) | async-done | bytes 4194336 | tf_op jit(solution)/shard_map/all_to_all | solution.py:81
  114.6 7.5 %copy.14 = bf16[4,256,8,256]{3,1,2,0:T(8,128)(2,1)} copy(bf16[4,256,8,256]{1,0,3,2:T(4,128)(2,1)} %bitcast.5) | data formatting | bytes 8388608 | tf_op jit(solution)/shard_map/all_to_all | solution.py:81
  122.1 12.4 %fusion.10 = f32[4,2048,256]{2,1,0:T(8,128)S(1)} fusion(bf16[4,2048,256]{2,1,0:T(8,128)(2,1)} %bitcast.34, bf16[1024,2048]{1,0:T(8,128)(2,1)} %get-tuple-element.13, bf16[1024,2048]{1,0:T(8,128)(2,1)} %get-tuple-element.14), kind=kOutput, calls=%fused_computation.25 | convolution fusion | flops 8606711808 | bytes 20971520 | tf_op jit(solution)/shard_map/fn,snc->sfc/dot_general | solution.py:78
  136.1 1.2 fusion.6
  137.4 1.9 copy-done.1
  139.3 2.4 collective-permute-start
  141.7 90.0 %collective-permute-done = bf16[4,2048,256]{2,1,0:T(8,128)(2,1)} collective-permute-done((bf16[4,2048,256]{2,1,0:T(8,128)(2,1)S(1)}, bf16[4,2048,256]{2,1,0:T(8,128)(2,1)}, u32[]{:S(2)}, u32[]{:S(2)}) %collective-permute-start) | collective-permute-done | bytes 4194336 | tf_op jit(solution)/shard_map/ppermute | solution.py:14
  231.7 7.3 %pad_maximum_fusion = bf16[4,2048,512]{2,1,0:T(8,128)(2,1)} fusion(bf16[4,2048,256]{2,1,0:T(8,128)(2,1)} %collective-permute-done, bf16[4,2048,256]{2,1,0:T(8,128)(2,1)} %copy-done.1), kind=kLoop, calls=%fused_computation.14 | loop fusion | flops 16777216 | bytes 16777216 | tf_op jit(solution)/shard_map/concatenate | solution.py:86
  239.0 15.3 %copy.15 = bf16[4,2048,512]{1,0,2:T(4,128)(2,1)} copy(bf16[4,2048,512]{2,1,0:T(8,128)(2,1)} %pad_maximum_fusion) | data formatting | bytes 16777216 | tf_op jit(solution)/shard_map/concatenate | solution.py:86
  254.3 13.3 %gather_fusion.1 = bf16[256,4,2048]{2,1,0:T(4,128)(2,1)} fusion(bf16[4,2048,512]{1,0,2:T(4,128)(2,1)} %copy.15, s32[1024]{0:T(1024)S(1)} %pad_clamp_fusion), kind=kCustom, calls=%fused_computation.1.clone | custom fusion | bytes 8389632 | tf_op jit(solution)/shard_map/jit(_take)/gather | solution.py:88
  267.6 13.3 %gather_fusion = bf16[256,4,2048]{2,1,0:T(4,128)(2,1)} fusion(bf16[4,2048,512]{1,0,2:T(4,128)(2,1)} %copy.15, s32[1024]{0:T(1024)S(1)} %pad_clamp_fusion.1), kind=kCustom, calls=%fused_computation.clone | custom fusion | bytes 8389632 | tf_op jit(solution)/shard_map/jit(_take)/gather | solution.py:87
  280.9 4.4 %select_bitcast_fusion = bf16[4,2048,256]{1,0,2:T(4,128)(2,1)S(1)} fusion(bf16[256,4,2048]{2,1,0:T(4,128)(2,1)} %gather_fusion.1, pred[256]{0:T(512)(128)(4,1)S(1)} %get-tuple-element.6), kind=kLoop, calls=%fused_computation.36 | loop fusion | flops 2097152 | bytes 8388864 | tf_op jit(solution)/shard_map/jit(_take)/select_n | solution.py:88
  285.3 1.9 select_bitcast_fusion.1
  287.3 6.4 %fusion.11 = (f32[4,1024,256]{1,0,2:T(4,128)}, f32[4,1024,256]{1,0,2:T(4,128)}) fusion(bf16[4,2048,256]{1,0,2:T(4,128)(2,1)S(1)} %select_bitcast_fusion, bf16[4,2048,256]{1,0,2:T(4,128)(2,1)S(1)} %select_bitcast_fusion.1), kind=kLoop, calls=%fused_computation.26 | loop fusion | flops 10485760 | bytes 16777216 | tf_op jit(solution)/shard_map/add | solution.py:56
  293.7 11.0 %maximum_reduce_fusion = f32[2048,256]{0,1:T(8,128)} fusion(f32[4,1024,256]{1,0,2:T(4,128)} %get-tuple-element.9, f32[4,1024,256]{1,0,2:T(4,128)} %get-tuple-element.8), kind=kLoop, calls=%fused_computation.15 | loop fusion | flops 3670016 | bytes 10485760 | tf_op jit(solution)/shard_map/reduce_sum | solution.py:89
  305.7 9.8 %cosine_multiply_fusion = (f32[512,1024]{1,0:T(8,128)S(1)}, f32[512,1024]{1,0:T(8,128)}) fusion(s32[512]{0:T(512)S(1)} %iota_add_fusion, f32[1024]{0:T(1024)S(1)} %get-tuple-element.15, f32[1024]{0:T(1024)S(1)} %get-tuple-element.16), kind=kLoop, calls=%fused_computation.45 | loop fusion | flops 8388608 | bytes 4204544 | tf_op jit(solution)/shard_map/mul | solution.py:34
  315.5 49.6 %all-gather.3.cloned.1.call-done = f32[8192,256]{0,1:T(8,128)} async-done(((f32[2048,256]{0,1:T(8,128)}), f32[8192,256]{0,1:T(8,128)}) %all-gather.3.cloned.1.call-update) | async-done | bytes 8388624 | tf_op jit(solution)/shard_map/all_gather | solution.py:91
  365.1 11.0 %reshape.68 = f32[4,2048,256]{1,0,2:T(4,128)} reshape(f32[8192,256]{0,1:T(8,128)} %all-gather.3.cloned.1.call-done) | data formatting | bytes 16777216 | tf_op jit(solution)/shard_map/all_gather | solution.py:91
  376.1 10.0 %reduce_sum.39 = f32[2048,256]{0,1:T(8,128)} reduce(f32[4,2048,256]{1,0,2:T(4,128)} %reshape.68, f32[]{:T(128)} %constant.63.clone.1), dimensions={0}, to_apply=%region_5.7 | reduce | flops 1572864 | bytes 10485764 | tf_op jit(solution)/shard_map/reduce_sum | solution.py:91
  386.1 5.7 %fusion.24 = bf16[512,256]{1,0:T(8,128)(2,1)S(1)} fusion(f32[2048,256]{0,1:T(8,128)} %reduce_sum.39, f32[512,1024]{1,0:T(8,128)} %get-tuple-element.11, f32[512,1024]{1,0:T(8,128)S(1)} %get-tuple-element.10), kind=kOutput, calls=%fused_computation.50 | convolution fusion | flops 3222405120 | bytes 6553600 | tf_op jit(solution)/shard_map/dot_general | solution.py:93
  392.2 23.4 %all_to_all.23 = bf16[8,80,512]{2,1,0:T(8,128)(2,1)S(1)} all-to-all(bf16[8,80,512]{2,1,0:T(8,128)(2,1)S(1)} %bitcast.35), channel_id=1, replica_groups=mesh['tile'=8,'win'=4] {'tile'}, dimensions={0} | all-to-all | bytes 1310720 | tf_op jit(solution)/shard_map/all_to_all | solution.py:103
  (29 shorter events, 3.8 us)
Async XLA Ops:
  14.0 100.6 %all-to-all-start = ((bf16[4,256,2048]{1,0,2:T(4,128)(2,1)}), bf16[4,256,2048]{1,0,2:T(4,128)(2,1)}, u32[]{:S(2)}, u32[]{:S(2)}) async-start(bf16[4,256,2048]{1,0,2:T(4,128)(2,1)} %copy.13), calls=%async_computation | async-start | bytes 8388608 | tf_op jit(solution)/shard_map/all_to_all | solution.py:81
  21.3 343.8 %all-gather.3.cloned.1.call-start = ((), (), s32[]{:S(2)}) async-start(), calls=%async_computation.2 | async-start | bytes 10485760 | tf_op jit(solution)/shard_map/all_gather | solution.py:91
  136.1 5.6 %copy-start.3 = (s32[256]{0:T(256)S(1)}, s32[256]{0:T(256)}, u32[]{:S(2)}) copy-start(s32[256]{0:T(256)} %param.7) | copy-start | bytes 3076
  136.1 5.6 %copy-start.4 = (s32[256]{0:T(256)S(1)}, s32[256]{0:T(256)}, u32[]{:S(2)}) copy-start(s32[256]{0:T(256)} %param.8) | copy-start | bytes 3076
  137.3 2.0 copy-start.1
  139.3 92.4 %collective-permute-start = (bf16[4,2048,256]{2,1,0:T(8,128)(2,1)S(1)}, bf16[4,2048,256]{2,1,0:T(8,128)(2,1)}, u32[]{:S(2)}, u32[]{:S(2)}) collective-permute-start(bf16[4,2048,256]{2,1,0:T(8,128)(2,1)S(1)} %fusion.6), channel_id=1, source_target_pairs={{4,0},{8,4},{12,8},{16,12},{20,16},{24,20},{28,24},{0,28},{5,1},{9... | collective-permute-start | bytes 12582920 | tf_op jit(solution)/shard_map/ppermute | solution.py:14
  280.9 4.4 %copy-start = (bf16[256,4,2048]{2,1,0:T(4,128)(2,1)S(1)}, bf16[256,4,2048]{2,1,0:T(4,128)(2,1)}, u32[]{:S(2)}) copy-start(bf16[256,4,2048]{2,1,0:T(4,128)(2,1)} %gather_fusion) | copy-start | bytes 12582916
  293.7 11.0 %copy-start.2 = (s32[256,1]{0,1:T(1,128)S(1)}, s32[256,1]{0,1:T(1,128)}, u32[]{:S(2)}) copy-start(s32[256,1]{0,1:T(1,128)} %param.9) | copy-start | bytes 3076
Sparse Core Ops, SparseCore 0:
  304.8 60.2 all-gather.2
